TPU v7x, 128 devices: a whole 4x4x4 slice. The times are simulated.
128 devices in a mesh: row: 4 (over z_hi, core), circ: 32 (over x, y, z_lo).
Axes of the slice: x: 4, y: 4, z: 4 (z_hi: 2, z_lo: 2; z = z_hi * 2 + z_lo), core: 2. Of those that a mesh axis runs over, the one named last changes fastest.
Arguments:
- flow_state: float32 [5, 64, 32, 4096], P(None, 'row', None, 'circ'), may hold values from -4 to 4
- velocity: float32 [3, 64, 32, 4096], P(None, 'row', None, 'circ'), may hold values from -3 to 3
- offsets: int32 [3, 3], replicated, may hold values from 0 to 4095, as said below
- passage_shift: int32 [4], replicated, may hold values from 0 to 31, as said below
- donor_step: int32 [4, 2, 4096], P('row', None, 'circ'), may hold values from 0 to 127
- donor_weight: float32 [4, 2, 4096], P('row', None, 'circ'), may hold values from 0.05 to 0.95
Outputs:
- updated_state: float32 [5, 64, 32, 4096], P(None, 'row', None, 'circ')
Inputs may be any that keep to these rules, and one draw needn't show every extreme that they name: Rotation offsets in cells; some interface takes the offset 4096 - 1 at some section in every draw, and with two or more interfaces some takes 0. `passage_shift`: passage index placed on device column 0 of each row; some row has 32 - 1 and some row 0 in every draw.
All inputs are finite; a program needn't handle non-finite values.
Results may differ from a plain program's by a relative error of at most 0.0003.
Values sent between devices are 32-bit elements; how exact they have to be, the bound alone decides.
No kernel may reach another device: no remote copies, remote signals or barrier semaphores. Data moves between devices by JAX's collectives and lax.ppermute only.
A program may use at most 128 MiB of HBM per device.

v0:
```python
import jax
import jax.numpy as jnp
from jax import lax
from jax.sharding import PartitionSpec as P

SMAG_COEF = 0.1
TIME_STEP = 0.25


def passed_along(value, axis, steps):
    count = lax.axis_size(axis)
    first, last = (max(0, -steps), min(count, count - steps))
    return lax.ppermute(value, axis, [(source, source + steps) for source in range(first, last)])


def extended(cells, sides, width):
    for axis, dim in sides:
        count = lax.axis_size(axis)
        head = lax.slice_in_dim(cells, 0, width, axis=dim)
        tail = lax.slice_in_dim(cells, cells.shape[dim] - width, cells.shape[dim], axis=dim)
        cells = jnp.concatenate(
            [
                lax.ppermute(tail, axis, [(i, (i + 1) % count) for i in range(count)]),
                cells,
                lax.ppermute(head, axis, [((i + 1) % count, i) for i in range(count)]),
            ],
            axis=dim,
        )
    return cells


def combine(fields, axial_ext, radial_ext, around_ext, velocity):
    d_axial = 0.5 * (axial_ext[:, 2:] - axial_ext[:, :-2])
    d_radial = 0.5 * (radial_ext[:, :, 2:] - radial_ext[:, :, :-2])
    d_around = 0.5 * (around_ext[..., 2:] - around_ext[..., :-2])
    laplace = (
        axial_ext[:, 2:]
        + axial_ext[:, :-2]
        + radial_ext[:, :, 2:]
        + radial_ext[:, :, :-2]
        + around_ext[..., 2:]
        + around_ext[..., :-2]
        - 6.0 * fields
    )
    strain = jnp.sum(d_axial[1:4] ** 2 + d_radial[1:4] ** 2 + d_around[1:4] ** 2, axis=0)
    eddy_visc = SMAG_COEF * jnp.sqrt(strain + 1.0)
    return eddy_visc * laplace - (
        velocity[0] * d_axial + velocity[1] * d_radial + velocity[2] * d_around
    )


def radial_pad(fields):
    return jnp.concatenate([fields[:, :, :1], fields, fields[:, :, -1:]], axis=2)


def axial_pad(fields, lower_ghost, upper_ghost):
    return jnp.concatenate([lower_ghost[:, None], fields, upper_ghost[:, None]], axis=1)


def local(flow_state, velocity, offsets, passage_shift, donor_step, donor_weight):
    row_count = lax.axis_size("row")
    loop_size = lax.axis_size("circ")
    row_id = lax.axis_index("row")
    column = lax.axis_index("circ")
    pitch_cells = flow_state.shape[-1]
    loop_cells = pitch_cells * loop_size
    passage = (column - passage_shift[row_id]) % loop_size
    lower_src = jnp.maximum(row_id - 1, 0)
    upper_src = jnp.minimum(row_id + 1, row_count - 1)
    lower_face = jnp.maximum(row_id - 1, 0)
    upper_face = jnp.minimum(row_id, row_count - 2)
    within = jnp.arange(pitch_cells, dtype=jnp.int32)

    def interface(face_plane, source_row, offset, donor_steps, weights):
        gathered = lax.all_gather(face_plane, "circ", axis=2, tiled=True)
        ordered = jnp.roll(gathered, -passage_shift[source_row] * pitch_cells, axis=2)
        donor_cols = (passage * pitch_cells + within + offset + donor_steps) % loop_cells
        next_cols = (donor_cols + 1) % loop_cells
        return weights * jnp.take(ordered, donor_cols, axis=2) + (1.0 - weights) * jnp.take(
            ordered, next_cols, axis=2
        )

    def evaluate(fields, section_index):
        first_plane = fields[:, 0]
        last_plane = fields[:, -1]
        from_below = passed_along(last_plane, "row", 1)
        from_above = passed_along(first_plane, "row", -1)
        low_offset = offsets[section_index, lower_face]
        high_offset = (loop_cells - offsets[section_index, upper_face]) % loop_cells
        lower_ghost = interface(
            from_below, lower_src, low_offset, donor_step[0, 0], donor_weight[0, 0]
        )
        upper_ghost = interface(
            from_above, upper_src, high_offset, donor_step[0, 1], donor_weight[0, 1]
        )
        lower_ghost = jnp.where(row_id == 0, first_plane, lower_ghost)
        upper_ghost = jnp.where(row_id == row_count - 1, last_plane, upper_ghost)
        around_ext = extended(fields, (("circ", 3),), 1)
        return combine(
            fields,
            axial_pad(fields, lower_ghost, upper_ghost),
            radial_pad(fields),
            around_ext,
            velocity,
        )

    section_one = flow_state + TIME_STEP * evaluate(flow_state, 0)
    section_two = 0.75 * flow_state + 0.25 * (section_one + TIME_STEP * evaluate(section_one, 1))
    return 1.0 / 3.0 * flow_state + 2.0 / 3.0 * (section_two + TIME_STEP * evaluate(section_two, 2))


def solution(mesh):
    placed = (
        P(None, "row", None, "circ"),
        P(None, "row", None, "circ"),
        P(),
        P(),
        P("row", None, "circ"),
        P("row", None, "circ"),
    )
    return jax.shard_map(
        local, mesh=mesh, in_specs=placed, out_specs=P(None, "row", None, "circ"), check_vma=False
    )
```

profile of v0, /device:TPU:0, one launch (start us, length us, event | category | flops | bytes accessed | tf_op | source)
XLA Modules:
  0.0 955.3 jit_solution(16857114506774725180)
XLA Ops:
  46.7 101.4 %all-gather.7.cloned.1.call-done = f32[5,32,4096]{2,1,0:T(8,128)} async-done(((f32[5,32,128]{2,1,0:T(8,128)}), f32[5,32,4096]{2,1,0:T(8,128)}) %all-gather.7.cloned.1.call-update) | async-done | bytes 2621456 | tf_op jit(solution)/shard_map/all_gather | solution.py:75
  152.8 9.6 %copy.302 = f32[5,32,4096]{1,0,2:T(8,128)} copy(f32[5,32,4096]{2,1,0:T(8,128)} %fusion.5) | data formatting | bytes 5242880
  162.4 7.2 gather_fusion.1
  171.5 7.4 gather_fusion
  180.6 101.7 %all-gather.9.cloned.1.call-done = f32[5,32,4096]{2,1,0:T(8,128)} async-done(((f32[5,32,128]{2,1,0:T(8,128)}), f32[5,32,4096]{2,1,0:T(8,128)}) %all-gather.9.cloned.1.call-update) | async-done | bytes 2621456 | tf_op jit(solution)/shard_map/all_gather | solution.py:75
  287.1 9.6 %copy.303 = f32[5,32,4096]{1,0,2:T(8,128)} copy(f32[5,32,4096]{2,1,0:T(8,128)} %fusion.4) | data formatting | bytes 5242880
  296.7 7.2 gather_fusion.2
  305.8 7.3 gather_fusion.3
  355.7 103.6 %all-gather.11.cloned.1.call-done = f32[5,32,4096]{2,1,0:T(8,128)} async-done(((f32[5,32,128]{2,1,0:T(8,128)}), f32[5,32,4096]{2,1,0:T(8,128)}) %all-gather.11.cloned.1.call-update) | async-done | bytes 2621456 | tf_op jit(solution)/shard_map/all_gather | solution.py:75
  463.9 9.6 %copy.308 = f32[5,32,4096]{1,0,2:T(8,128)} copy(f32[5,32,4096]{2,1,0:T(8,128)} %fusion.3) | data formatting | bytes 5242880
  473.6 7.3 gather_fusion.5
  482.7 7.4 gather_fusion.4
  491.9 102.5 %all-gather.13.cloned.1.call-done = f32[5,32,4096]{2,1,0:T(8,128)} async-done(((f32[5,32,128]{2,1,0:T(8,128)}), f32[5,32,4096]{2,1,0:T(8,128)}) %all-gather.13.cloned.1.call-update) | async-done | bytes 2621456 | tf_op jit(solution)/shard_map/all_gather | solution.py:75
  599.1 9.6 %copy.309 = f32[5,32,4096]{1,0,2:T(8,128)} copy(f32[5,32,4096]{2,1,0:T(8,128)} %fusion.2) | data formatting | bytes 5242880
  608.8 7.2 gather_fusion.6
  617.8 7.2 gather_fusion.7
  668.5 104.5 %all-gather.15.cloned.1.call-done = f32[5,32,4096]{2,1,0:T(8,128)} async-done(((f32[5,32,128]{2,1,0:T(8,128)}), f32[5,32,4096]{2,1,0:T(8,128)}) %all-gather.15.cloned.1.call-update) | async-done | bytes 2621456 | tf_op jit(solution)/shard_map/all_gather | solution.py:75
  777.7 9.6 %copy.312 = f32[5,32,4096]{1,0,2:T(8,128)} copy(f32[5,32,4096]{2,1,0:T(8,128)} %fusion.1) | data formatting | bytes 5242880
  787.3 7.4 gather_fusion.9
  796.5 7.4 gather_fusion.8
  805.7 101.5 %all-gather.17.cloned.1.call-done = f32[5,32,4096]{2,1,0:T(8,128)} async-done(((f32[5,32,128]{2,1,0:T(8,128)}), f32[5,32,4096]{2,1,0:T(8,128)}) %all-gather.17.cloned.1.call-update) | async-done | bytes 2621456 | tf_op jit(solution)/shard_map/all_gather | solution.py:75
  911.9 9.6 %copy.313 = f32[5,32,4096]{1,0,2:T(8,128)} copy(f32[5,32,4096]{2,1,0:T(8,128)} %fusion) | data formatting | bytes 5242880
  921.5 7.2 gather_fusion.10
  930.6 7.2 gather_fusion.11
  (180 shorter events, 176.8 us)
Async XLA Ops:
  6.5 141.6 %all-gather.7.cloned.1.call-start = ((), (), s32[]{:S(2)}) async-start(), calls=%async_computation | async-start | bytes 2703360 | tf_op jit(solution)/shard_map/all_gather | solution.py:75
  7.5 3.2 collective-permute-start
  11.3 271.0 %all-gather.9.cloned.1.call-start = ((), (), s32[]{:S(2)}) async-start(), calls=%async_computation.1 | async-start | bytes 2703360 | tf_op jit(solution)/shard_map/all_gather | solution.py:75
  11.4 7.8 collective-permute-start.1
  19.8 439.5 %all-gather.11.cloned.1.call-start = ((), (), s32[]{:S(2)}) async-start(), calls=%async_computation.2 | async-start | bytes 2703360 | tf_op jit(solution)/shard_map/all_gather | solution.py:75
  25.1 17.9 %collective-permute-start.2 = (f32[5,16,32,1]{2,1,3,0:T(8,128)S(1)}, f32[5,16,32,1]{2,1,3,0:T(8,128)}, u32[]{:S(2)}, u32[]{:S(2)}) collective-permute-start(f32[5,16,32,1]{2,1,3,0:T(8,128)S(1)} %copy.304), channel_id=1, source_target_pairs={{1,0},{2,1},{3,2},{4,3},{5,4},{6,5},{7,6},{8,7},{9,8},{10,9},{11,1... | collective-permute-start | bytes 30728 | tf_op jit(solution)/shard_map/ppermute | solution.py:25
  31.9 12.4 %collective-permute-start.3 = (f32[5,16,32,1]{2,1,3,0:T(8,128)}, f32[5,16,32,1]{2,1,3,0:T(8,128)}, u32[]{:S(2)}, u32[]{:S(2)}) collective-permute-start(f32[5,16,32,1]{2,1,3,0:T(8,128)} %copy.305), channel_id=1, source_target_pairs={{0,1},{1,2},{2,3},{3,4},{4,5},{5,6},{6,7},{7,8},{8,9},{9,10},{10,1... | collective-permute-start | bytes 30728 | tf_op jit(solution)/shard_map/ppermute | solution.py:23
  44.3 271.7 %copy-start.3 = (f32[5,16,32,1]{3,2,1,0:T(8,128)}, f32[5,16,32,1]{3,2,1,0:T(8,128)S(1)}, u32[]{:S(2)}) copy-start(f32[5,16,32,1]{3,2,1,0:T(8,128)S(1)} %copy.269) | copy-start | bytes 30724
  296.7 18.2 %copy-start.14 = (pred[128]{0:T(512)(128)(4,1)S(1)}, pred[128]{0:T(512)(128)(4,1)}, u32[]{:S(2)}) copy-start(pred[128]{0:T(512)(128)(4,1)} %get-tuple-element.25) | copy-start | bytes 388
  296.7 18.2 %copy-start.15 = (pred[128]{0:T(512)(128)(4,1)S(1)}, pred[128]{0:T(512)(128)(4,1)}, u32[]{:S(2)}) copy-start(pred[128]{0:T(512)(128)(4,1)} %get-tuple-element.94) | copy-start | bytes 388
  296.7 18.2 %copy-start.24 = (pred[128]{0:T(512)(128)(4,1)S(1)}, pred[128]{0:T(512)(128)(4,1)}, u32[]{:S(2)}) copy-start(pred[128]{0:T(512)(128)(4,1)} %get-tuple-element.79) | copy-start | bytes 388
  296.7 18.2 %copy-start.25 = (pred[128]{0:T(512)(128)(4,1)S(1)}, pred[128]{0:T(512)(128)(4,1)}, u32[]{:S(2)}) copy-start(pred[128]{0:T(512)(128)(4,1)} %get-tuple-element.81) | copy-start | bytes 388
  322.4 305.6 %copy-start.1 = (f32[5,16,32,128]{3,2,1,0:T(8,128)}, f32[5,16,32,128]{3,2,1,0:T(8,128)S(1)}, u32[]{:S(2)}) copy-start(f32[5,16,32,128]{3,2,1,0:T(8,128)S(1)} %multiply_add_fusion.2) | copy-start | bytes 3932164
  322.4 3.3 collective-permute-start.4
  325.7 268.7 %all-gather.13.cloned.1.call-start = ((), (), s32[]{:S(2)}) async-start(), calls=%async_computation.3 | async-start | bytes 2703360 | tf_op jit(solution)/shard_map/all_gather | solution.py:75
  325.8 6.3 collective-permute-start.5
  332.2 440.9 %all-gather.15.cloned.1.call-start = ((), (), s32[]{:S(2)}) async-start(), calls=%async_computation.4 | async-start | bytes 2703360 | tf_op jit(solution)/shard_map/all_gather | solution.py:75
  338.1 6.5 collective-permute-start.6
  344.5 8.7 collective-permute-start.7
  635.0 3.3 collective-permute-start.8
  638.3 268.8 %all-gather.17.cloned.1.call-start = ((), (), s32[]{:S(2)}) async-start(), calls=%async_computation.5 | async-start | bytes 2703360 | tf_op jit(solution)/shard_map/all_gather | solution.py:75
  638.4 6.9 collective-permute-start.9
  651.0 6.6 collective-permute-start.10
  657.5 8.7 collective-permute-start.11
  (26 other events, 272.8 us)
Sparse Core Ops, SparseCore 0:
  11.4 136.6 all-gather.6
  149.7 132.6 all-gather.8
  325.9 133.3 all-gather.10
  460.7 133.6 all-gather.12
  638.4 134.5 all-gather.14
  774.4 132.6 all-gather.16
where the time goes:
time: 958 us; the launch traced here: 955 us
  waiting for transfers between devices  635 us (66%)
  local copies, waits for them, and re-layouts  207 us (22%)
  other arithmetic  57.5 us (6%)
  starting transfers between devices  37.3 us (4%)
  between operations  18 us (2%)
    all_gather x6, waiting for transfers between devices, interface(): gathered = lax.all_gather(face_plane, 'circ', axis=2, tiled=True)  615 us
    unnamed x72, local copies, waits for them, and re-layouts  66.2 us
    gather x12, local copies, waits for them, and re-layouts, interface(): jnp.take(ordered, donor_cols, axis=2)  54.6 us
    gather x12, local copies, waits for them, and re-layouts, interface(): jnp.take(ordered, next_cols, axis=2)  54.6 us
    concatenate x6, other arithmetic, interface(): jnp.roll(gathered, -passage_shift[source_row] * pitch_cells, axis=2)  28.1 us
    ppermute x6, starting transfers between devices, passed_along(): lax.ppermute(value, axis, [(source, source + steps) for source in range(f...  23.2 us
  transfers between devices with their start and end apart: 18, of which 14 were waited for; matrix products, arithmetic and copies ran while one was open for 15% of the time, Pallas kernels for 0%

commit v1 on v0

--- a/solution.py
+++ b/solution.py
@@ -1,3 +1,4 @@
+import functools
 import jax
 import jax.numpy as jnp
 from jax import lax
@@ -5,6 +6,14 @@
 
 SMAG_COEF = 0.1
 TIME_STEP = 0.25
+
+
+def state_masks_now(matrix, axis_name):
+    now = lax.all_to_all(jnp.stack(lax.axis_size(axis_name) * [matrix], axis=0), axis_name, 0, 0)
+    return jnp.concatenate(now, axis=2)
+
+
+post_table = functools.partial(state_masks_now, axis_name="circ")
 
 
 def passed_along(value, axis, steps):
@@ -72,7 +81,7 @@
     within = jnp.arange(pitch_cells, dtype=jnp.int32)
 
     def interface(face_plane, source_row, offset, donor_steps, weights):
-        gathered = lax.all_gather(face_plane, "circ", axis=2, tiled=True)
+        gathered = post_table(face_plane)
         ordered = jnp.roll(gathered, -passage_shift[source_row] * pitch_cells, axis=2)
         donor_cols = (passage * pitch_cells + within + offset + donor_steps) % loop_cells
         next_cols = (donor_cols + 1) % loop_cells

time: 958 us -> 481 us (0.50)
  waiting for transfers between devices: 635 us -> 108 us
  starting transfers between devices: 37.3 us -> 84.7 us
  local copies, waits for them, and re-layouts: 207 us -> 229 us
  between operations: 18 us -> 4.67 us
  other arithmetic: 57.5 us -> 45.8 us
    all_gather x6 -> x0, waiting for transfers between devices: 615 us -> none  [interface(): gathered = lax.all_gather(face_plane, 'circ', axis=2, tiled=True)]
    all_to_all x0 -> x6, waiting for transfers between devices: none -> 60.6 us  [state_masks_now(): lax.all_to_all(jnp.stack(lax.axis_size(axis_name) * [matrix], axis=0), ax...]
    all_to_all x0 -> x6, starting transfers between devices: none -> 43.2 us  [state_masks_now(): lax.all_to_all(jnp.stack(lax.axis_size(axis_name) * [matrix], axis=0), ax...]
    ppermute x3, waiting for transfers between devices: 0.01 us -> 19 us  [extended(): lax.ppermute(head, axis, [((i + 1) % count, i) for i in range(count)])]
    another operation x0 -> x6, local copies, waits for them, and re-layouts: none -> 12.7 us  [state_masks_now(): jnp.stack(lax.axis_size(axis_name) * [matrix], axis=0)]
    reshape x0 -> x6, local copies, waits for them, and re-layouts: none -> 12.1 us  [state_masks_now(): return jnp.concatenate(now, axis=2)]
    concatenate x6, other arithmetic: 28.1 us -> 17.7 us  [interface(): jnp.roll(gathered, -passage_shift[source_row] * pitch_cells, axis=2)]
    unnamed x72 -> x70, local copies, waits for them, and re-layouts: 66.2 us -> 65.1 us
  transfers between devices with their start and end apart: 18 -> 18, of which waited for: 14 -> 12; matrix products, arithmetic and copies ran while one was open for 15% -> 30% of each run, Pallas kernels for 0% -> 0%
where the time goes in v1:
time: 481 us; the launch traced here: 472 us
  local copies, waits for them, and re-layouts  229 us (48%)
  waiting for transfers between devices  108 us (22%)
  starting transfers between devices  84.7 us (18%)
  other arithmetic  45.8 us (10%)
    unnamed x70, local copies, waits for them, and re-layouts  65.1 us
    all_to_all x6, waiting for transfers between devices, state_masks_now(): lax.all_to_all(jnp.stack(lax.axis_size(axis_name) * [matrix], axis=0), ax...  60.6 us
    gather x12, local copies, waits for them, and re-layouts, interface(): jnp.take(ordered, donor_cols, axis=2)  54.5 us
    gather x12, local copies, waits for them, and re-layouts, interface(): jnp.take(ordered, next_cols, axis=2)  54.5 us
    all_to_all x6, starting transfers between devices, state_masks_now(): lax.all_to_all(jnp.stack(lax.axis_size(axis_name) * [matrix], axis=0), ax...  43.2 us
    ppermute x6, starting transfers between devices, passed_along(): lax.ppermute(value, axis, [(source, source + steps) for source in range(f...  23.1 us
    ppermute x3, waiting for transfers between devices, extended(): lax.ppermute(tail, axis, [(i, (i + 1) % count) for i in range(count)])  20.3 us
    ppermute x3, waiting for transfers between devices, extended(): lax.ppermute(head, axis, [((i + 1) % count, i) for i in range(count)])  19 us
  transfers between devices with their start and end apart: 18, of which 12 were waited for; matrix products, arithmetic and copies ran while one was open for 30% of the time, Pallas kernels for 0%

profile of v1, /device:TPU:0, one launch (start us, length us, event | category | flops | bytes accessed | tf_op | source)
XLA Modules:
  0.0 471.7 jit_solution(6113354366230017445)
XLA Ops:
  5.9 9.0 %all-to-all-start = ((f32[32,5,32,128]{3,2,1,0:T(8,128)}), f32[32,5,32,128]{3,2,1,0:T(8,128)}, u32[]{:S(2)}, u32[]{:S(2)}) async-start(f32[32,5,32,128]{3,2,1,0:T(8,128)} %stack.12), calls=%async_computation | async-start | bytes 5242880 | tf_op jit(solution)/shard_map/all_to_all | solution.py:12
  37.9 11.6 %all-to-all-done = f32[32,5,32,128]{3,2,1,0:T(8,128)} async-done(((f32[32,5,32,128]{3,2,1,0:T(8,128)}), f32[32,5,32,128]{3,2,1,0:T(8,128)}, u32[]{:S(2)}, u32[]{:S(2)}) %all-to-all-start) | async-done | bytes 2621472 | tf_op jit(solution)/shard_map/all_to_all | solution.py:12
  68.7 9.7 %copy.349 = f32[5,32,4096]{1,0,2:T(8,128)} copy(f32[5,32,4096]{2,1,0:T(8,128)} %fusion.5) | data formatting | bytes 5242880
  87.4 7.3 %gather_fusion = f32[128,5,32]{2,1,0:T(8,128)} fusion(f32[5,32,4096]{1,0,2:T(8,128)} %copy.349, s32[1024]{0:T(1024)} %pad_clamp_fusion.11), kind=kCustom, calls=%fused_computation.clone | custom fusion | bytes 164352 | tf_op jit(solution)/shard_map/jit(_take)/gather | solution.py:88
  101.5 9.7 %copy.350 = f32[5,32,4096]{1,0,2:T(8,128)} copy(f32[5,32,4096]{2,1,0:T(8,128)} %fusion.4) | data formatting | bytes 5242880
  120.2 7.3 %gather_fusion.3 = f32[128,5,32]{2,1,0:T(8,128)} fusion(f32[5,32,4096]{1,0,2:T(8,128)} %copy.350, s32[1024]{0:T(1024)} %pad_clamp_fusion.8), kind=kCustom, calls=%fused_computation.3.clone | custom fusion | bytes 164352 | tf_op jit(solution)/shard_map/jit(_take)/gather | solution.py:88
  143.0 8.4 %all-to-all-start.2 = ((f32[32,5,32,128]{3,2,1,0:T(8,128)}), f32[32,5,32,128]{3,2,1,0:T(8,128)}, u32[]{:S(2)}, u32[]{:S(2)}) async-start(f32[32,5,32,128]{3,2,1,0:T(8,128)} %stack.14), calls=%async_computation.2 | async-start | bytes 5242880 | tf_op jit(solution)/shard_map/all_to_all | solution.py:12
  159.2 24.5 %all-to-all-done.2 = f32[32,5,32,128]{3,2,1,0:T(8,128)} async-done(((f32[32,5,32,128]{3,2,1,0:T(8,128)}), f32[32,5,32,128]{3,2,1,0:T(8,128)}, u32[]{:S(2)}, u32[]{:S(2)}) %all-to-all-start.2) | async-done | bytes 2621472 | tf_op jit(solution)/shard_map/all_to_all | solution.py:12
  206.2 9.5 %collective-permute-done.6 = f32[5,16,32,1]{2,1,3,0:T(8,128)} collective-permute-done((f32[5,16,32,1]{2,1,3,0:T(8,128)S(1)}, f32[5,16,32,1]{2,1,3,0:T(8,128)}, u32[]{:S(2)}, u32[]{:S(2)}) %collective-permute-start.6) | collective-permute-done | bytes 10272 | tf_op jit(solution)/shard_map/ppermute | solution.py:34
  218.2 10.2 %collective-permute-done.7 = f32[5,16,32,1]{2,1,3,0:T(8,128)} collective-permute-done((f32[5,16,32,1]{2,1,3,0:T(8,128)}, f32[5,16,32,1]{2,1,3,0:T(8,128)}, u32[]{:S(2)}, u32[]{:S(2)}) %collective-permute-start.7) | collective-permute-done | bytes 10272 | tf_op jit(solution)/shard_map/ppermute | solution.py:32
  235.7 9.7 %copy.355 = f32[5,32,4096]{1,0,2:T(8,128)} copy(f32[5,32,4096]{2,1,0:T(8,128)} %fusion.3) | data formatting | bytes 5242880
  245.4 7.3 %gather_fusion.5 = f32[128,5,32]{2,1,0:T(8,128)} fusion(f32[5,32,4096]{1,0,2:T(8,128)} %copy.355, s32[1024]{0:T(1024)} %pad_clamp_fusion.6), kind=kCustom, calls=%fused_computation.5.clone | custom fusion | bytes 164352 | tf_op jit(solution)/shard_map/jit(_take)/gather | solution.py:88
  254.5 7.3 %gather_fusion.4 = f32[128,5,32]{2,1,0:T(8,128)} fusion(f32[5,32,4096]{1,0,2:T(8,128)} %copy.355, s32[1024]{0:T(1024)} %pad_clamp_fusion.7), kind=kCustom, calls=%fused_computation.4.clone | custom fusion | bytes 164352 | tf_op jit(solution)/shard_map/jit(_take)/gather | solution.py:88
  268.6 9.7 %copy.356 = f32[5,32,4096]{1,0,2:T(8,128)} copy(f32[5,32,4096]{2,1,0:T(8,128)} %fusion.2) | data formatting | bytes 5242880
  278.3 7.2 %gather_fusion.6 = f32[128,5,32]{2,1,0:T(8,128)} fusion(f32[5,32,4096]{1,0,2:T(8,128)} %copy.356, s32[1024]{0:T(1024)S(1)} %pad_clamp_fusion.5), kind=kCustom, calls=%fused_computation.6.clone | custom fusion | bytes 164352 | tf_op jit(solution)/shard_map/jit(_take)/gather | solution.py:88
  309.7 8.0 %all-to-all-start.4 = ((f32[32,5,32,128]{3,2,1,0:T(8,128)}), f32[32,5,32,128]{3,2,1,0:T(8,128)}, u32[]{:S(2)}, u32[]{:S(2)}) async-start(f32[32,5,32,128]{3,2,1,0:T(8,128)} %stack.16), calls=%async_computation.4 | async-start | bytes 5242880 | tf_op jit(solution)/shard_map/all_to_all | solution.py:12
  325.5 24.6 %all-to-all-done.4 = f32[32,5,32,128]{3,2,1,0:T(8,128)} async-done(((f32[32,5,32,128]{3,2,1,0:T(8,128)}), f32[32,5,32,128]{3,2,1,0:T(8,128)}, u32[]{:S(2)}, u32[]{:S(2)}) %all-to-all-start.4) | async-done | bytes 2621472 | tf_op jit(solution)/shard_map/all_to_all | solution.py:12
  372.5 9.5 %collective-permute-done.10 = f32[5,16,32,1]{2,1,3,0:T(8,128)} collective-permute-done((f32[5,16,32,1]{2,1,3,0:T(8,128)S(1)}, f32[5,16,32,1]{2,1,3,0:T(8,128)}, u32[]{:S(2)}, u32[]{:S(2)}) %collective-permute-start.10) | collective-permute-done | bytes 10272 | tf_op jit(solution)/shard_map/ppermute | solution.py:34
  384.4 10.2 %collective-permute-done.11 = f32[5,16,32,1]{2,1,3,0:T(8,128)} collective-permute-done((f32[5,16,32,1]{2,1,3,0:T(8,128)}, f32[5,16,32,1]{2,1,3,0:T(8,128)}, u32[]{:S(2)}, u32[]{:S(2)}) %collective-permute-start.11) | collective-permute-done | bytes 10272 | tf_op jit(solution)/shard_map/ppermute | solution.py:32
  402.0 9.7 %copy.359 = f32[5,32,4096]{1,0,2:T(8,128)} copy(f32[5,32,4096]{2,1,0:T(8,128)} %fusion.1) | data formatting | bytes 5242880
  411.7 7.3 %gather_fusion.9 = f32[128,5,32]{2,1,0:T(8,128)} fusion(f32[5,32,4096]{1,0,2:T(8,128)} %copy.359, s32[1024]{0:T(1024)} %pad_clamp_fusion.2), kind=kCustom, calls=%fused_computation.9.clone | custom fusion | bytes 164352 | tf_op jit(solution)/shard_map/jit(_take)/gather | solution.py:88
  420.8 7.3 %gather_fusion.8 = f32[128,5,32]{2,1,0:T(8,128)} fusion(f32[5,32,4096]{1,0,2:T(8,128)} %copy.359, s32[1024]{0:T(1024)} %pad_clamp_fusion.3), kind=kCustom, calls=%fused_computation.8.clone | custom fusion | bytes 164352 | tf_op jit(solution)/shard_map/jit(_take)/gather | solution.py:88
  434.9 9.7 %copy.360 = f32[5,32,4096]{1,0,2:T(8,128)} copy(f32[5,32,4096]{2,1,0:T(8,128)} %fusion) | data formatting | bytes 5242880
  444.6 7.2 %gather_fusion.10 = f32[128,5,32]{2,1,0:T(8,128)} fusion(f32[5,32,4096]{1,0,2:T(8,128)} %copy.360, s32[1024]{0:T(1024)S(1)} %pad_clamp_fusion.1), kind=kCustom, calls=%fused_computation.10.clone | custom fusion | bytes 164352 | tf_op jit(solution)/shard_map/jit(_take)/gather | solution.py:88
  (181 shorter events, 225.1 us)
Async XLA Ops:
  0.9 3.2 collective-permute-start
  5.9 43.5 %all-to-all-start = ((f32[32,5,32,128]{3,2,1,0:T(8,128)}), f32[32,5,32,128]{3,2,1,0:T(8,128)}, u32[]{:S(2)}, u32[]{:S(2)}) async-start(f32[32,5,32,128]{3,2,1,0:T(8,128)} %stack.12), calls=%async_computation | async-start | bytes 5242880 | tf_op jit(solution)/shard_map/all_to_all | solution.py:12
  15.0 22.9 %collective-permute-start.1 = (f32[5,32,128]{2,1,0:T(8,128)S(1)}, f32[5,32,128]{2,1,0:T(8,128)S(1)}, u32[]{:S(2)}, u32[]{:S(2)}) collective-permute-start(f32[5,32,128]{2,1,0:T(8,128)S(1)} %get-tuple-element.60), channel_id=1, source_target_pairs={{0,32},{32,64},{64,96},{1,33},{33,65},{65,97},{2,34},{34,66},{66,9... | collective-permute-start | bytes 245768 | tf_op jit(solution)/shard_map/ppermute | solution.py:22
  24.0 35.9 %collective-permute-start.2 = (f32[5,16,32,1]{2,1,3,0:T(8,128)S(1)}, f32[5,16,32,1]{2,1,3,0:T(8,128)}, u32[]{:S(2)}, u32[]{:S(2)}) collective-permute-start(f32[5,16,32,1]{2,1,3,0:T(8,128)S(1)} %copy.351), channel_id=1, source_target_pairs={{1,0},{2,1},{3,2},{4,3},{5,4},{6,5},{7,6},{8,7},{9,8},{10,9},{11,1... | collective-permute-start | bytes 30728 | tf_op jit(solution)/shard_map/ppermute | solution.py:34
  30.9 30.3 %collective-permute-start.3 = (f32[5,16,32,1]{2,1,3,0:T(8,128)}, f32[5,16,32,1]{2,1,3,0:T(8,128)}, u32[]{:S(2)}, u32[]{:S(2)}) collective-permute-start(f32[5,16,32,1]{2,1,3,0:T(8,128)} %copy.352), channel_id=1, source_target_pairs={{0,1},{1,2},{2,3},{3,4},{4,5},{5,6},{6,7},{7,8},{8,9},{9,10},{10,1... | collective-permute-start | bytes 30728 | tf_op jit(solution)/shard_map/ppermute | solution.py:32
  51.3 45.3 %all-to-all-start.1 = ((f32[32,5,32,128]{3,2,1,0:T(8,128)}), f32[32,5,32,128]{3,2,1,0:T(8,128)}, u32[]{:S(2)}, u32[]{:S(2)}) async-start(f32[32,5,32,128]{3,2,1,0:T(8,128)} %stack.13), calls=%async_computation.1 | async-start | bytes 5242880 | tf_op jit(solution)/shard_map/all_to_all | solution.py:12
  61.2 69.2 %copy-start.3 = (f32[5,16,32,1]{3,2,1,0:T(8,128)}, f32[5,16,32,1]{3,2,1,0:T(8,128)S(1)}, u32[]{:S(2)}) copy-start(f32[5,16,32,1]{3,2,1,0:T(8,128)S(1)} %copy.312) | copy-start | bytes 30724
  111.2 18.2 %copy-start.17 = (pred[128]{0:T(512)(128)(4,1)S(1)}, pred[128]{0:T(512)(128)(4,1)}, u32[]{:S(2)}) copy-start(pred[128]{0:T(512)(128)(4,1)} %get-tuple-element.25) | copy-start | bytes 388
  111.2 18.2 %copy-start.18 = (pred[128]{0:T(512)(128)(4,1)S(1)}, pred[128]{0:T(512)(128)(4,1)}, u32[]{:S(2)}) copy-start(pred[128]{0:T(512)(128)(4,1)} %get-tuple-element.94) | copy-start | bytes 388
  111.2 18.2 %copy-start.27 = (pred[128]{0:T(512)(128)(4,1)S(1)}, pred[128]{0:T(512)(128)(4,1)}, u32[]{:S(2)}) copy-start(pred[128]{0:T(512)(128)(4,1)} %get-tuple-element.79) | copy-start | bytes 388
  111.2 18.2 %copy-start.28 = (pred[128]{0:T(512)(128)(4,1)S(1)}, pred[128]{0:T(512)(128)(4,1)}, u32[]{:S(2)}) copy-start(pred[128]{0:T(512)(128)(4,1)} %get-tuple-element.81) | copy-start | bytes 388
  136.8 160.7 %copy-start.1 = (f32[5,16,32,128]{3,2,1,0:T(8,128)}, f32[5,16,32,128]{3,2,1,0:T(8,128)S(1)}, u32[]{:S(2)}) copy-start(f32[5,16,32,128]{3,2,1,0:T(8,128)S(1)} %multiply_add_fusion.2) | copy-start | bytes 3932164
  136.9 4.3 collective-permute-start.4
  143.0 40.7 %all-to-all-start.2 = ((f32[32,5,32,128]{3,2,1,0:T(8,128)}), f32[32,5,32,128]{3,2,1,0:T(8,128)}, u32[]{:S(2)}, u32[]{:S(2)}) async-start(f32[32,5,32,128]{3,2,1,0:T(8,128)} %stack.14), calls=%async_computation.2 | async-start | bytes 5242880 | tf_op jit(solution)/shard_map/all_to_all | solution.py:12
  152.0 7.2 %collective-permute-start.5 = (f32[5,32,128]{2,1,0:T(8,128)S(1)}, f32[5,32,128]{2,1,0:T(8,128)}, u32[]{:S(2)}, u32[]{:S(2)}) collective-permute-start(f32[5,32,128]{2,1,0:T(8,128)S(1)} %get-tuple-element.49), channel_id=1, source_target_pairs={{0,32},{32,64},{64,96},{1,33},{33,65},{65,97},{2,34},{34,66},{66,9... | collective-permute-start | bytes 245768 | tf_op jit(solution)/shard_map/ppermute | solution.py:22
  186.4 77.3 %all-to-all-start.3 = ((f32[32,5,32,128]{3,2,1,0:T(8,128)}), f32[32,5,32,128]{3,2,1,0:T(8,128)}, u32[]{:S(2)}, u32[]{:S(2)}) async-start(f32[32,5,32,128]{3,2,1,0:T(8,128)} %stack.15), calls=%async_computation.3 | async-start | bytes 5242880 | tf_op jit(solution)/shard_map/all_to_all | solution.py:12
  197.5 18.3 %collective-permute-start.6 = (f32[5,16,32,1]{2,1,3,0:T(8,128)S(1)}, f32[5,16,32,1]{2,1,3,0:T(8,128)}, u32[]{:S(2)}, u32[]{:S(2)}) collective-permute-start(f32[5,16,32,1]{2,1,3,0:T(8,128)S(1)} %copy.327), channel_id=1, source_target_pairs={{1,0},{2,1},{3,2},{4,3},{5,4},{6,5},{7,6},{8,7},{9,8},{10,9},{11,1... | collective-permute-start | bytes 30728 | tf_op jit(solution)/shard_map/ppermute | solution.py:34
  206.0 22.3 %collective-permute-start.7 = (f32[5,16,32,1]{2,1,3,0:T(8,128)}, f32[5,16,32,1]{2,1,3,0:T(8,128)}, u32[]{:S(2)}, u32[]{:S(2)}) collective-permute-start(f32[5,16,32,1]{2,1,3,0:T(8,128)} %copy.329), channel_id=1, source_target_pairs={{0,1},{1,2},{2,3},{3,4},{4,5},{5,6},{6,7},{7,8},{8,9},{9,10},{10,1... | collective-permute-start | bytes 30728 | tf_op jit(solution)/shard_map/ppermute | solution.py:32
  304.5 3.3 collective-permute-start.8
  309.7 40.4 %all-to-all-start.4 = ((f32[32,5,32,128]{3,2,1,0:T(8,128)}), f32[32,5,32,128]{3,2,1,0:T(8,128)}, u32[]{:S(2)}, u32[]{:S(2)}) async-start(f32[32,5,32,128]{3,2,1,0:T(8,128)} %stack.16), calls=%async_computation.4 | async-start | bytes 5242880 | tf_op jit(solution)/shard_map/all_to_all | solution.py:12
  318.2 7.2 %collective-permute-start.9 = (f32[5,32,128]{2,1,0:T(8,128)S(1)}, f32[5,32,128]{2,1,0:T(8,128)}, u32[]{:S(2)}, u32[]{:S(2)}) collective-permute-start(f32[5,32,128]{2,1,0:T(8,128)S(1)} %get-tuple-element.38), channel_id=1, source_target_pairs={{0,32},{32,64},{64,96},{1,33},{33,65},{65,97},{2,34},{34,66},{66,9... | collective-permute-start | bytes 245768 | tf_op jit(solution)/shard_map/ppermute | solution.py:22
  352.7 77.3 %all-to-all-start.5 = ((f32[32,5,32,128]{3,2,1,0:T(8,128)}), f32[32,5,32,128]{3,2,1,0:T(8,128)}, u32[]{:S(2)}, u32[]{:S(2)}) async-start(f32[32,5,32,128]{3,2,1,0:T(8,128)} %stack.17), calls=%async_computation.5 | async-start | bytes 5242880 | tf_op jit(solution)/shard_map/all_to_all | solution.py:12
  363.7 18.3 %collective-permute-start.10 = (f32[5,16,32,1]{2,1,3,0:T(8,128)S(1)}, f32[5,16,32,1]{2,1,3,0:T(8,128)}, u32[]{:S(2)}, u32[]{:S(2)}) collective-permute-start(f32[5,16,32,1]{2,1,3,0:T(8,128)S(1)} %copy.343), channel_id=1, source_target_pairs={{1,0},{2,1},{3,2},{4,3},{5,4},{6,5},{7,6},{8,7},{9,8},{10,9},{11,1... | collective-permute-start | bytes 30728 | tf_op jit(solution)/shard_map/ppermute | solution.py:34
  372.3 22.3 %collective-permute-start.11 = (f32[5,16,32,1]{2,1,3,0:T(8,128)}, f32[5,16,32,1]{2,1,3,0:T(8,128)}, u32[]{:S(2)}, u32[]{:S(2)}) collective-permute-start(f32[5,16,32,1]{2,1,3,0:T(8,128)} %copy.345), channel_id=1, source_target_pairs={{0,1},{1,2},{2,3},{3,4},{4,5},{5,6},{6,7},{7,8},{8,9},{9,10},{10,1... | collective-permute-start | bytes 30728 | tf_op jit(solution)/shard_map/ppermute | solution.py:32
  (25 other events, 249.8 us)
